TPU v7x, 32 devices: a whole 2x2x4 slice. The times are simulated.
32 devices in a mesh: req: 4 (over y, x), cand: 8 (over z, core).
Axes of the slice: x: 2, y: 2, z: 4, core: 2. Of those that a mesh axis runs over, the one named last changes fastest.
Arguments:
- table: bfloat16 [32768, 256], P('req'), may hold values from -6 to 6
- history_shard: int32 [4, 1024, 1], P('req', 'cand'), may hold values from 0 to 3; in each aligned block of 128 rows (0 to 127, 128 to 255, ..., all dimensions but the last counted through in order) at most 128 rows name the same one
- history_row: int32 [4, 1024], P('req', 'cand'), may hold values from 0 to 8191
- candidate_shard: int32 [4, 2048, 1], P('req', 'cand'), may hold values from 0 to 3; in each aligned block of 256 rows (0 to 255, 256 to 511, ..., all dimensions but the last counted through in order) at most 192 rows name the same one
- candidate_row: int32 [4, 2048], P('req', 'cand'), may hold values from 0 to 8191
- history_length: int32 [4], P('req'), may hold values from 128 to 1024, as said below
- w_query: bfloat16 [256, 256], replicated, may hold values from -0.375 to 0.375
- w_key: bfloat16 [256, 256], replicated, may hold values from -0.375 to 0.375
- w_value: bfloat16 [256, 256], replicated, may hold values from -0.375 to 0.375
- tower_in: bfloat16 [512, 1024], replicated, may hold values from -0.25 to 0.25
- tower_out: bfloat16 [1024], replicated, may hold values from -0.1875 to 0.1875
Outputs:
- logits: float32 [4, 2048], P('req', 'cand')
Inputs may be any that keep to these rules, and one draw needn't show every extreme that they name: `history_shard`: among the 128 events of one request that one device holds, at most 128 name the same table shard, a bound that some block reaches. `candidate_shard`: among the 256 candidates of one request that one device holds, at most 192 name the same table shard, a bound that some block reaches. `history_length`: some request has all 1024 events live.
All inputs are finite; a program needn't handle non-finite values.
Results may differ from a plain program's by a relative error of at most 0.004.
Values may be sent and summed in bfloat16 or wider, within the bound.
No kernel may reach another device: no remote copies, remote signals or barrier semaphores. Data moves between devices by JAX's collectives and lax.ppermute only.
A program may use at most 64 MiB of HBM per device.

v0:
```python
import math
import jax
import jax.numpy as jnp
from jax import lax
from jax.sharding import PartitionSpec as P

HEADS = 4


def slot_index(shard_ids, n_dest, slot_count, first_slot):
    onehot = (shard_ids[:, None] == jnp.arange(n_dest, dtype=jnp.int32)[None, :]).astype(jnp.int32)
    before = jnp.cumsum(onehot, axis=0) - onehot
    rank = jnp.sum(before * onehot, axis=1)
    return shard_ids * slot_count + first_slot + rank


def body(
    table,
    history_shard,
    history_row,
    candidate_shard,
    candidate_row,
    history_length,
    w_query,
    w_key,
    w_value,
    tower_in,
    tower_out,
):
    n_dest = lax.axis_size("req")
    d_model = table.shape[1]
    hist_shards = history_shard[0, :, 0]
    cand_shards = candidate_shard[0, :, 0]
    hist_dev = hist_shards.shape[0]
    cand_dev = cand_shards.shape[0]
    hist_cap = 4 * hist_dev // n_dest
    cand_cap = 3 * cand_dev // n_dest
    slot_count = hist_cap + cand_cap
    hist_slot = slot_index(hist_shards, n_dest, slot_count, 0)
    cand_slot = slot_index(cand_shards, n_dest, slot_count, hist_cap)
    wanted = jnp.zeros((n_dest * slot_count,), jnp.int32)
    wanted = wanted.at[hist_slot].set(history_row[0]).at[cand_slot].set(candidate_row[0])
    wanted = wanted.reshape(n_dest, slot_count)
    fetched = jnp.take(
        table, lax.all_to_all(wanted, "req", split_axis=0, concat_axis=0, tiled=True), axis=0
    )
    replies = lax.all_to_all(fetched, "req", split_axis=0, concat_axis=0, tiled=True)
    flat_rows = replies.reshape(n_dest * slot_count, d_model)
    hist_emb = jnp.take(flat_rows, hist_slot, axis=0)
    cand_emb = jnp.take(flat_rows, cand_slot, axis=0)
    head_size = d_model // HEADS
    scale_factor = 1.0 / math.sqrt(head_size)
    length = history_length[0]
    w_pair = jnp.concatenate([w_key, w_value], axis=1)
    query_row_matrix = jnp.dot(cand_emb, w_query, preferred_element_type=jnp.float32).astype(
        jnp.bfloat16
    )
    query_row_matrix = query_row_matrix.reshape(cand_dev, HEADS, head_size)
    pair_local = jnp.dot(hist_emb, w_pair, preferred_element_type=jnp.float32).astype(jnp.bfloat16)
    pair_rows = lax.all_gather(pair_local, "cand", axis=0, tiled=True)
    count = pair_rows.shape[0]
    key_portion_slice = pair_rows[:, :d_model].reshape(count, HEADS, head_size)
    value_portion_slice = pair_rows[:, d_model:].reshape(count, HEADS, head_size)
    score_matrix = (
        jnp.einsum(
            "zun,aun->zua", query_row_matrix, key_portion_slice, preferred_element_type=jnp.float32
        )
        * scale_factor
    )
    live_mask = jnp.arange(count, dtype=jnp.int32) < length
    gate_weights = jnp.where(
        live_mask[None, None, :], jax.nn.sigmoid(score_matrix), jnp.float32(0.0)
    ).astype(jnp.bfloat16)
    weighted_sum = jnp.einsum(
        "bgo,ogl->bgl", gate_weights, value_portion_slice, preferred_element_type=jnp.float32
    )
    attended = (
        (weighted_sum / jnp.sqrt(length.astype(jnp.float32)))
        .reshape(cand_dev, d_model)
        .astype(jnp.bfloat16)
    )
    pre_act = jnp.dot(cand_emb, tower_in[:d_model], preferred_element_type=jnp.float32) + jnp.dot(
        attended, tower_in[d_model:], preferred_element_type=jnp.float32
    )
    hidden = jax.nn.silu(pre_act).astype(jnp.bfloat16)
    return jnp.dot(hidden, tower_out, preferred_element_type=jnp.float32)[None, :]


def solution(mesh):
    placed = (
        P("req", None),
        P("req", "cand", None),
        P("req", "cand"),
        P("req", "cand", None),
        P("req", "cand"),
        P("req"),
        P(),
        P(),
        P(),
        P(),
        P(),
    )
    return jax.shard_map(
        body, mesh=mesh, in_specs=placed, out_specs=P("req", "cand"), check_vma=False
    )
```

profile of v0, /device:TPU:0, one launch (start us, length us, event | category | flops | bytes accessed | tf_op | source)
XLA Modules:
  0.0 80.8 jit_solution(6493712422928214452)
XLA Ops:
  6.5 0.0 copy-start
  6.5 0.7 compare_convert_fusion
  7.3 1.2 %reduce-window.6 = s32[4,2,128]{2,1,0:T(2,128)S(1)} reduce-window(s32[4,2,128]{2,1,0:T(2,128)S(1)} %compare_convert_fusion, s32[]{:T(128)} %constant.41.clone.1), window={size=1x1x128 pad=0_0x0_0x127_0}, to_apply=%region_0.0 | reduce-window | flops 130048 | bytes 8196 | tf_op jit(solution)/shard_map/reduce-window
  8.5 0.1 slice.30
  8.5 0.1 copy.19
  8.7 0.1 copy.20
  8.8 0.1 add_bitcast_fusion
  8.9 0.7 fusion.24
  9.6 0.7 compare_select_fusion.2
  10.2 0.7 fusion.18
  11.0 0.2 reduce_window_sum.28
  11.2 0.8 %select_reduce_fusion = s32[128]{0:T(128)S(1)} fusion(s32[128,4]{1,0:T(8,128)S(1)} %reduce_window_sum.28, s32[128]{0:T(128)} %bitcast.86), kind=kLoop, calls=%fused_computation.25 | loop fusion | flops 2432 | bytes 3072 | tf_op jit(solution)/shard_map/reduce_sum | solution.py:13
  12.0 0.7 fusion.27
  12.7 1.1 %scatter_custom_fusion = s32[1280]{0:T(1024)S(1)} fusion(s32[128]{0:T(128)S(1)} %fusion.27, s32[128]{0:T(128)} %bitcast.88, s32[]{:T(128)} %constant.41.clone.1), kind=kCustom, calls=%fused_computation.44 | custom fusion | bytes 5632 | tf_op jit(solution)/shard_map/scatter | solution.py:42
  13.8 1.6 %scatter_fusion = s32[1280]{0:T(1024)S(1)} fusion(s32[1280]{0:T(1024)S(1)} %scatter_custom_fusion, s32[256]{0:T(256)S(1)} %bitcast.81, s32[256]{0:T(256)} %bitcast.87), kind=kCustom, calls=%fused_computation.4 | custom fusion | bytes 4096 | tf_op jit(solution)/shard_map/scatter | solution.py:42
  15.4 0.1 all_to_all.13
  15.4 9.6 %all_to_all.20 = s32[4,1,320]{2,1,0:T(1,128)S(1)} all-to-all(s32[4,1,320]{2,1,0:T(1,128)S(1)} %all_to_all.13), channel_id=1, replica_groups=mesh['req'=4,'cand'=8] {'req'}, dimensions={0} | all-to-all | bytes 10240 | tf_op jit(solution)/shard_map/all_to_all | solution.py:45
  25.1 0.1 reshape.156
  25.2 0.0 copy-start.3
  25.2 0.0 copy-start.5
  25.2 0.0 copy-start.6
  25.2 0.0 copy-start.4
  25.2 0.0 copy-start.2
  25.3 5.9 %gather_fusion = bf16[1280,256]{1,0:T(8,128)(2,1)S(1)} fusion(bf16[8192,256]{1,0:T(8,128)(2,1)} %param.11, s32[2048]{0:T(1024)S(1)} %pad_clamp_fusion), kind=kCustom, calls=%fused_computation | custom fusion | bytes 1315840 | tf_op jit(solution)/shard_map/jit(_take)/gather | solution.py:44
  31.2 0.0 copy-start.1
  31.2 1.1 %broadcast_select_fusion = bf16[4,320,256]{2,1,0:T(8,128)(2,1)} fusion(bf16[4,320,256]{2,1,0:T(8,128)(2,1)S(1)} %bitcast.74, pred[4,320]{1,0:T(4,128)(4,1)S(1)} %compare_and_fusion), kind=kLoop, calls=%fused_computation.15 | loop fusion | flops 327680 | bytes 1312000 | tf_op jit(solution)/shard_map/jit(_take)/select_n | solution.py:44
  32.3 3.5 %all-to-all-start.1 = ((bf16[4,320,256]{2,1,0:T(8,128)(2,1)}), bf16[4,320,256]{2,1,0:T(8,128)(2,1)S(1)}, u32[]{:S(2)}, u32[]{:S(2)}) async-start(bf16[4,320,256]{2,1,0:T(8,128)(2,1)} %broadcast_select_fusion), calls=%async_computation.1 | async-start | bytes 1310720 | tf_op jit(solution)/shard_map/all_to_all | solution.py:47
  35.8 0.0 all-gather.2.cloned.1.call-start
  35.9 0.0 copy-done.3
  35.9 8.1 %all-to-all-done.1 = bf16[4,320,256]{2,1,0:T(8,128)(2,1)S(1)} async-done(((bf16[4,320,256]{2,1,0:T(8,128)(2,1)}), bf16[4,320,256]{2,1,0:T(8,128)(2,1)S(1)}, u32[]{:S(2)}, u32[]{:S(2)}) %all-to-all-start.1) | async-done | bytes 655392 | tf_op jit(solution)/shard_map/all_to_all | solution.py:47
  44.0 0.8 %gather_fusion.2 = bf16[128,256]{1,0:T(8,128)(2,1)S(1)} fusion(bf16[1280,256]{1,0:T(8,128)(2,1)S(1)} %bitcast.72, s32[1024]{0:T(1024)S(1)} %pad_clamp_fusion.1), kind=kCustom, calls=%fused_computation.2 | custom fusion | bytes 131584 | tf_op jit(solution)/shard_map/jit(_take)/gather | solution.py:49
  44.9 0.0 copy-done.5
  44.9 0.0 copy-done.6
  44.9 0.9 %convolution_convert_fusion.1 = bf16[128,512]{1,0:T(8,128)(2,1)} fusion(bf16[256,256]{1,0:T(8,128)(2,1)S(1)} %copy-done.5, bf16[256,256]{1,0:T(8,128)(2,1)S(1)} %copy-done.6, bf16[128,256]{1,0:T(8,128)(2,1)S(1)} %gather_fusion.2, pred[128]{0:T(512)(128)(4,1)S(1)} %compare_and_fusion.1), kind=kOutput, calls=%fused_computation.10 | convolution fusion | flops 34177024 | bytes 458880 | tf_op jit(solution)/shard_map/dot_general | solution.py:59
  45.8 0.0 all-gather.2.cloned.1.call-update
  46.5 0.0 copy-done.4
  46.6 0.0 copy-done.2
  46.6 1.2 %gather_fusion.1 = bf16[256,256]{1,0:T(8,128)(2,1)S(1)} fusion(bf16[1280,256]{1,0:T(8,128)(2,1)S(1)} %bitcast.73, s32[1024]{0:T(1024)S(1)} %pad_clamp_fusion.2), kind=kCustom, calls=%fused_computation.1 | custom fusion | bytes 263168 | tf_op jit(solution)/shard_map/jit(_take)/gather | solution.py:50
  47.7 0.0 copy-done
  47.7 0.3 convolution_convert_fusion
  48.0 0.0 copy-done.1
  48.1 0.3 fusion.12
  48.4 19.9 %all-gather.2.cloned.1.call-done = bf16[1024,512]{1,0:T(8,128)(2,1)} async-done(((bf16[128,512]{1,0:T(8,128)(2,1)}), bf16[1024,512]{1,0:T(8,128)(2,1)}) %all-gather.2.cloned.1.call-update) | async-done | bytes 1048592 | tf_op jit(solution)/shard_map/all_gather | solution.py:60
  68.3 1.3 %fusion.36 = (bf16[1024,256]{1,0:T(8,128)(2,1)S(1)}, bf16[1024,256]{1,0:T(8,128)(2,1)S(1)}) fusion(bf16[1024,512]{1,0:T(8,128)(2,1)} %all-gather.2.cloned.1.call-done), kind=kLoop, calls=%fused_computation.64 | loop fusion | bytes 2097152 | tf_op jit(solution)/shard_map/slice | solution.py:62
  69.6 0.2 copy.22
  69.8 0.2 copy.21
  70.0 1.6 %fusion.5 = bf16[4,64,256]{2,1,0:T(8,128)(2,1)S(1)} fusion(bf16[1024,4,64]{0,2,1:T(8,128)(2,1)S(1)} %bitcast.76, bf16[1024,4,64]{0,2,1:T(8,128)(2,1)S(1)} %bitcast.75, bf16[256,4,64]{0,2,1:T(8,128)(2,1)S(1)} %bitcast.77, pred[1024]{0:T(1024)(128)(4,1)S(1)} %iota_compare_fusion.1, f32[]{:T(128)S(6)} %sqrt.3), kind=kOutput, calls=%fused_computation.12 | convolution fusion | flops 274857984 | bytes 1311748 | tf_op jit(solution)/shard_map/bgo,ogl->bgl/dot_general | solution.py:74
  71.6 2.3 %fusion.8 = f32[1,256]{1,0:T(1,128)} fusion(bf16[1024,1]{0,1:T(2,128)(2,1)S(1)} %reshape.195, f32[256,1024]{1,0:T(8,128)S(1)} %fusion.12, bf16[256,256]{0,1:T(8,128)(2,1)S(1)} %bitcast.89, bf16[512,1024]{1,0:T(8,128)(2,1)} %param.20), kind=kOutput, calls=%fused_computation.14 | convolution fusion | flops 136314880 | bytes 1707008 | tf_op jit(solution)/shard_map/dot_general | solution.py:86
  (11 shorter events, 0.1 us)
Async XLA Ops:
  6.5 41.2 %copy-start = (bf16[256,256]{1,0:T(8,128)(2,1)S(1)}, bf16[256,256]{1,0:T(8,128)(2,1)}, u32[]{:S(2)}) copy-start(bf16[256,256]{1,0:T(8,128)(2,1)} %param.17) | copy-start | bytes 393220
  25.2 10.7 %copy-start.3 = (s32[1,128,1]{1,2,0:T(1,128)S(1)}, s32[1,128,1]{1,2,0:T(1,128)}, u32[]{:S(2)}) copy-start(s32[1,128,1]{1,2,0:T(1,128)} %param.12) | copy-start | bytes 1540
  25.2 19.7 %copy-start.5 = (bf16[256,256]{1,0:T(8,128)(2,1)S(1)}, bf16[256,256]{1,0:T(8,128)(2,1)}, u32[]{:S(2)}) copy-start(bf16[256,256]{1,0:T(8,128)(2,1)} %param.19) | copy-start | bytes 393220
  25.2 19.7 %copy-start.6 = (bf16[256,256]{1,0:T(8,128)(2,1)S(1)}, bf16[256,256]{1,0:T(8,128)(2,1)}, u32[]{:S(2)}) copy-start(bf16[256,256]{1,0:T(8,128)(2,1)} %param.18) | copy-start | bytes 393220
  25.2 21.3 %copy-start.4 = (bf16[1024]{0:T(1024)(128)(2,1)S(1)}, bf16[1024]{0:T(1024)(128)(2,1)}, u32[]{:S(2)}) copy-start(bf16[1024]{0:T(1024)(128)(2,1)} %param.21) | copy-start | bytes 6148
  25.2 21.3 %copy-start.2 = (s32[1,256,1]{1,2,0:T(1,128)S(1)}, s32[1,256,1]{1,2,0:T(1,128)}, u32[]{:S(2)}) copy-start(s32[1,256,1]{1,2,0:T(1,128)} %param.14) | copy-start | bytes 3076
  31.2 16.8 %copy-start.1 = (bf16[512,1024]{1,0:T(8,128)(2,1)S(1)}, bf16[512,1024]{1,0:T(8,128)(2,1)}, u32[]{:S(2)}) copy-start(bf16[512,1024]{1,0:T(8,128)(2,1)} %param.20) | copy-start | bytes 3145732
  32.3 11.7 %all-to-all-start.1 = ((bf16[4,320,256]{2,1,0:T(8,128)(2,1)}), bf16[4,320,256]{2,1,0:T(8,128)(2,1)S(1)}, u32[]{:S(2)}, u32[]{:S(2)}) async-start(bf16[4,320,256]{2,1,0:T(8,128)(2,1)} %broadcast_select_fusion), calls=%async_computation.1 | async-start | bytes 1310720 | tf_op jit(solution)/shard_map/all_to_all | solution.py:47
  35.8 32.5 %all-gather.2.cloned.1.call-start = ((), (), s32[]{:S(2)}) async-start(), calls=%async_computation.2 | async-start | bytes 1179648 | tf_op jit(solution)/shard_map/all_gather | solution.py:60
Sparse Core Ops, SparseCore 0:
  45.9 22.3 all-gather.1
where the time goes:
time: 81.1 us; the launch traced here: 80.8 us
  waiting for transfers between devices  28.1 us (35%)
  between operations  14.3 us (18%)
  local copies, waits for them, and re-layouts  12.8 us (16%)
  blocking collectives  9.64 us (12%)
  other arithmetic  6.98 us (9%)
  matrix products  5.39 us (7%)
  starting transfers between devices  3.52 us (4%)
    all_gather x1, waiting for transfers between devices, body(): pair_rows = lax.all_gather(pair_local, 'cand', axis=0, tiled=True)  19.9 us
    all_to_all x1, blocking collectives, body(): lax.all_to_all(wanted, 'req', split_axis=0, concat_axis=0, tiled=True)  9.64 us
    all_to_all x1, waiting for transfers between devices, body(): lax.all_to_all(fetched, 'req', split_axis=0, concat_axis=0, tiled=True)  8.15 us
    gather x1, local copies, waits for them, and re-layouts, body(): jnp.take(table, lax.all_to_all(wanted, 'req', split_axis=0, concat_axis=0...  5.95 us
    all_to_all x1, starting transfers between devices, body(): lax.all_to_all(fetched, 'req', split_axis=0, concat_axis=0, tiled=True)  3.48 us
    scatter x2, local copies, waits for them, and re-layouts, body(): wanted.at[hist_slot].set(history_row[0]).at[cand_slot].set(candidate_row[0])  2.7 us
    dot_general x1, matrix products, body(): jnp.dot(hidden, tower_out, preferred_element_type=jnp.float32)[None, :]  2.27 us
  transfers between devices with their start and end apart: 2, of which 2 were waited for; matrix products, arithmetic and copies ran while one was open for 2% of the time, Pallas kernels for 0%

commit v1 on v0

--- a/solution.py
+++ b/solution.py
@@ -5,6 +5,17 @@
 from jax.sharding import PartitionSpec as P
 
 HEADS = 4
+
+
+def in_blocks(array, dim, size):
+    before, after = (array.shape[:dim], array.shape[dim + 1 :])
+    return jnp.moveaxis(array.reshape(*before, size, -1, *after), dim, 0)
+
+
+def joined_along(pieces, dim):
+    shape = list(pieces.shape[1:])
+    shape[dim] *= pieces.shape[0]
+    return jnp.moveaxis(pieces, 0, dim).reshape(shape)
 
 
 def slot_index(shard_ids, n_dest, slot_count, first_slot):
@@ -44,7 +55,14 @@
     fetched = jnp.take(
         table, lax.all_to_all(wanted, "req", split_axis=0, concat_axis=0, tiled=True), axis=0
     )
-    replies = lax.all_to_all(fetched, "req", split_axis=0, concat_axis=0, tiled=True)
+    size, here = (lax.axis_size("req"), lax.axis_index("req"))
+    pieces = in_blocks(fetched, 0, size)
+    outs = [pieces[here]]
+    for step in range(1, size):
+        sent = pieces[here ^ step]
+        outs.append(lax.ppermute(sent, "req", [(i, i ^ step) for i in range(size)]))
+    pieces = jnp.stack(outs)[here ^ jnp.arange(size)]
+    replies = joined_along(pieces, 0)
     flat_rows = replies.reshape(n_dest * slot_count, d_model)
     hist_emb = jnp.take(flat_rows, hist_slot, axis=0)
     cand_emb = jnp.take(flat_rows, cand_slot, axis=0)

time: 81.1 us -> 78.4 us (0.967)
  blocking collectives: 9.64 us -> 0 us
  starting transfers between devices: 3.52 us -> 8.72 us
  local copies, waits for them, and re-layouts: 12.8 us -> 14 us
    all_to_all x1 -> x0, blocking collectives: 9.64 us -> none  [body(): lax.all_to_all(wanted, 'req', split_axis=0, concat_axis=0, tiled=True)]
    ppermute x0 -> x3, waiting for transfers between devices: none -> 4.8 us  [body(): outs.append(lax.ppermute(sent, 'req', [(i, i ^ step) for i in range(size)]))]
    all_to_all x1, waiting for transfers between devices: 8.15 us -> 3.99 us  [body(): lax.all_to_all(wanted, 'req', split_axis=0, concat_axis=0, tiled=True)]
    ppermute x0 -> x3, starting transfers between devices: none -> 3.55 us  [body(): outs.append(lax.ppermute(sent, 'req', [(i, i ^ step) for i in range(size)]))]
    all_to_all x1, starting transfers between devices: 3.48 us -> 5.16 us  [body(): lax.all_to_all(wanted, 'req', split_axis=0, concat_axis=0, tiled=True)]
    select_n x2, other arithmetic: 1.1 us -> 0.27 us  [body(): jnp.take(table, lax.all_to_all(wanted, 'req', split_axis=0, concat_axis=0...]
  transfers between devices with their start and end apart: 2 -> 5, of which waited for: 2 -> 4; matrix products, arithmetic and copies ran while one was open for 2% -> 3% of each run, Pallas kernels for 0% -> 0%
where the time goes in v1:
time: 78.4 us; the launch traced here: 78 us
  waiting for transfers between devices  28.7 us (37%)
  between operations  14.3 us (18%)
  local copies, waits for them, and re-layouts  14 us (18%)
  starting transfers between devices  8.72 us (11%)
  other arithmetic  6.9 us (9%)
  matrix products  5.39 us (7%)
    all_gather x1, waiting for transfers between devices, body(): pair_rows = lax.all_gather(pair_local, 'cand', axis=0, tiled=True)  19.9 us
    gather x1, local copies, waits for them, and re-layouts, body(): jnp.take(table, lax.all_to_all(wanted, 'req', split_axis=0, concat_axis=0...  5.86 us
    all_to_all x1, starting transfers between devices, body(): lax.all_to_all(wanted, 'req', split_axis=0, concat_axis=0, tiled=True)  5.16 us
    ppermute x3, waiting for transfers between devices, body(): outs.append(lax.ppermute(sent, 'req', [(i, i ^ step) for i in range(size)]))  4.8 us
    all_to_all x1, waiting for transfers between devices, body(): lax.all_to_all(wanted, 'req', split_axis=0, concat_axis=0, tiled=True)  3.99 us
    ppermute x3, starting transfers between devices, body(): outs.append(lax.ppermute(sent, 'req', [(i, i ^ step) for i in range(size)]))  3.55 us
    scatter x2, local copies, waits for them, and re-layouts, body(): wanted.at[hist_slot].set(history_row[0]).at[cand_slot].set(candidate_row[0])  2.7 us
    dot_general x1, matrix products, body(): jnp.dot(hidden, tower_out, preferred_element_type=jnp.float32)[None, :]  2.27 us
  transfers between devices with their start and end apart: 5, of which 4 were waited for; matrix products, arithmetic and copies ran while one was open for 3% of the time, Pallas kernels for 0%

profile of v1, /device:TPU:0, one launch (start us, length us, event | category | flops | bytes accessed | tf_op | source)
XLA Modules:
  0.0 78.0 jit_solution(2912909123871484966)
XLA Ops:
  6.5 0.7 compare_convert_fusion
  7.3 1.2 %reduce-window.6 = s32[4,2,128]{2,1,0:T(2,128)S(1)} reduce-window(s32[4,2,128]{2,1,0:T(2,128)S(1)} %compare_convert_fusion, s32[]{:T(128)} %constant.37.clone.1), window={size=1x1x128 pad=0_0x0_0x127_0}, to_apply=%region_0.0 | reduce-window | flops 130048 | bytes 8196 | tf_op jit(solution)/shard_map/reduce-window
  8.5 0.1 slice.32
  8.5 0.1 copy.19
  8.7 0.1 copy.20
  8.8 0.1 add_bitcast_fusion
  8.9 0.7 fusion.24
  9.6 0.7 compare_select_fusion.2
  10.2 0.7 fusion.18
  11.0 0.2 reduce_window_sum.28
  11.2 0.8 %select_reduce_fusion = s32[128]{0:T(128)S(1)} fusion(s32[128,4]{1,0:T(8,128)S(1)} %reduce_window_sum.28, s32[128]{0:T(128)} %bitcast.98), kind=kLoop, calls=%fused_computation.28 | loop fusion | flops 2432 | bytes 3072 | tf_op jit(solution)/shard_map/reduce_sum | solution.py:24
  12.0 0.7 fusion.27
  12.7 1.1 %scatter_custom_fusion = s32[1280]{0:T(1024)S(1)} fusion(s32[128]{0:T(128)S(1)} %fusion.27, s32[128]{0:T(128)} %bitcast.100, s32[]{:T(128)} %constant.37.clone.1), kind=kCustom, calls=%fused_computation.48 | custom fusion | bytes 5632 | tf_op jit(solution)/shard_map/scatter | solution.py:53
  13.8 1.6 %scatter_fusion = s32[1280]{0:T(1024)S(1)} fusion(s32[1280]{0:T(1024)S(1)} %scatter_custom_fusion, s32[256]{0:T(256)S(1)} %bitcast.93, s32[256]{0:T(256)} %bitcast.99), kind=kCustom, calls=%fused_computation.5 | custom fusion | bytes 4096 | tf_op jit(solution)/shard_map/scatter | solution.py:53
  15.4 0.7 all_to_all.10
  16.0 5.2 %all-to-all-start = ((s32[4,1,320]{2,1,0:T(1,128)}), s32[4,1,320]{2,1,0:T(1,128)S(1)}, u32[]{:S(2)}, u32[]{:S(2)}) async-start(s32[4,1,320]{2,1,0:T(1,128)} %all_to_all.10), calls=%async_computation | async-start | bytes 12288 | tf_op jit(solution)/shard_map/all_to_all | solution.py:56
  21.2 0.7 compare_and_fusion.1
  21.9 4.0 %all-to-all-done = s32[4,1,320]{2,1,0:T(1,128)S(1)} async-done(((s32[4,1,320]{2,1,0:T(1,128)}), s32[4,1,320]{2,1,0:T(1,128)S(1)}, u32[]{:S(2)}, u32[]{:S(2)}) %all-to-all-start) | async-done | bytes 5152 | tf_op jit(solution)/shard_map/all_to_all | solution.py:56
  25.9 0.1 reshape.176
  26.0 5.9 %gather_fusion = bf16[1280,256]{1,0:T(8,128)(2,1)S(1)} fusion(bf16[8192,256]{1,0:T(8,128)(2,1)} %param.11, s32[2048]{0:T(1024)S(1)} %pad_clamp_fusion), kind=kCustom, calls=%fused_computation | custom fusion | bytes 1315840 | tf_op jit(solution)/shard_map/jit(_take)/gather | solution.py:55
  31.9 0.0 copy-start.4
  31.9 0.0 copy-start.5
  31.9 0.0 copy-start.3
  31.9 0.0 copy-start.2
  31.9 0.0 copy-start.1
  32.0 0.2 broadcast_select_fusion
  32.2 0.1 dynamic-slice_bitcast_fusion
  32.3 0.6 collective-permute-start.2
  32.9 1.5 %collective-permute-start.1 = (bf16[1,320,256]{2,1,0:T(8,128)(2,1)S(1)}, bf16[1,320,256]{2,1,0:T(8,128)(2,1)S(1)}, u32[]{:S(2)}, u32[]{:S(2)}) collective-permute-start(bf16[1,320,256]{2,1,0:T(8,128)(2,1)S(1)} %get-tuple-element.9), channel_id=1, source_target_pairs={{0,16},{8,24},{16,0},{24,8},{1,17},{9,25},{17,1},{25,9},{2,18},{10... | collective-permute-start | bytes 491528 | tf_op jit(solution)/shard_map/ppermute | solution.py:63
  34.4 1.4 %collective-permute-start = (bf16[1,320,256]{2,1,0:T(8,128)(2,1)S(1)}, bf16[1,320,256]{2,1,0:T(8,128)(2,1)S(1)}, u32[]{:S(2)}, u32[]{:S(2)}) collective-permute-start(bf16[1,320,256]{2,1,0:T(8,128)(2,1)S(1)} %get-tuple-element.10), channel_id=1, source_target_pairs={{0,8},{8,0},{16,24},{24,16},{1,9},{9,1},{17,25},{25,17},{2,10},{10... | collective-permute-start | bytes 491528 | tf_op jit(solution)/shard_map/ppermute | solution.py:63
  35.8 3.8 %collective-permute-done.2 = bf16[1,320,256]{2,1,0:T(8,128)(2,1)S(1)} collective-permute-done((bf16[1,320,256]{2,1,0:T(8,128)(2,1)S(1)}, bf16[1,320,256]{2,1,0:T(8,128)(2,1)S(1)}, u32[]{:S(2)}, u32[]{:S(2)}) %collective-permute-start.2) | collective-permute-done | bytes 163872 | tf_op jit(solution)/shard_map/ppermute | solution.py:63
  39.7 1.0 %collective-permute-done.1 = bf16[1,320,256]{2,1,0:T(8,128)(2,1)S(1)} collective-permute-done((bf16[1,320,256]{2,1,0:T(8,128)(2,1)S(1)}, bf16[1,320,256]{2,1,0:T(8,128)(2,1)S(1)}, u32[]{:S(2)}, u32[]{:S(2)}) %collective-permute-start.1) | collective-permute-done | bytes 163872 | tf_op jit(solution)/shard_map/ppermute | solution.py:63
  40.6 0.0 collective-permute-done
  40.6 0.1 maximum_bitcast_fusion
  40.7 0.6 gather_fusion.1
  41.3 0.8 %gather_fusion.3 = bf16[128,256]{1,0:T(8,128)(2,1)S(1)} fusion(bf16[1280,256]{1,0:T(8,128)(2,1)S(1)} %bitcast.81, s32[1024]{0:T(1024)S(1)} %pad_clamp_fusion.1), kind=kCustom, calls=%fused_computation.3 | custom fusion | bytes 131584 | tf_op jit(solution)/shard_map/jit(_take)/gather | solution.py:67
  42.2 0.0 copy-done.4
  42.2 0.9 %convolution_convert_fusion.1 = bf16[128,512]{1,0:T(8,128)(2,1)} fusion(bf16[256,256]{1,0:T(8,128)(2,1)S(1)} %copy-done.4, bf16[256,256]{1,0:T(8,128)(2,1)S(1)} %copy-done.5, bf16[128,256]{1,0:T(8,128)(2,1)S(1)} %gather_fusion.3, pred[128]{0:T(512)(128)(4,1)S(1)} %compare_and_fusion.1), kind=kOutput, calls=%fused_computation.11 | convolution fusion | flops 34177024 | bytes 458880 | tf_op jit(solution)/shard_map/dot_general | solution.py:77
  43.1 0.0 all-gather.2.cloned.1.call-update
  43.9 1.2 %gather_fusion.2 = bf16[256,256]{1,0:T(8,128)(2,1)S(1)} fusion(bf16[1280,256]{1,0:T(8,128)(2,1)S(1)} %bitcast.82, s32[1024]{0:T(1024)S(1)} %pad_clamp_fusion.2), kind=kCustom, calls=%fused_computation.2 | custom fusion | bytes 263168 | tf_op jit(solution)/shard_map/jit(_take)/gather | solution.py:68
  45.0 0.3 convolution_convert_fusion
  45.3 0.3 fusion.12
  45.7 19.9 %all-gather.2.cloned.1.call-done = bf16[1024,512]{1,0:T(8,128)(2,1)} async-done(((bf16[128,512]{1,0:T(8,128)(2,1)}), bf16[1024,512]{1,0:T(8,128)(2,1)}) %all-gather.2.cloned.1.call-update) | async-done | bytes 1048592 | tf_op jit(solution)/shard_map/all_gather | solution.py:78
  65.6 1.3 %fusion.37 = (bf16[1024,256]{1,0:T(8,128)(2,1)S(1)}, bf16[1024,256]{1,0:T(8,128)(2,1)S(1)}) fusion(bf16[1024,512]{1,0:T(8,128)(2,1)} %all-gather.2.cloned.1.call-done), kind=kLoop, calls=%fused_computation.73 | loop fusion | bytes 2097152 | tf_op jit(solution)/shard_map/slice | solution.py:80
  66.9 0.2 copy.22
  67.1 0.2 copy.21
  67.3 1.6 %fusion.5 = bf16[4,64,256]{2,1,0:T(8,128)(2,1)S(1)} fusion(bf16[1024,4,64]{0,2,1:T(8,128)(2,1)S(1)} %bitcast.85, bf16[1024,4,64]{0,2,1:T(8,128)(2,1)S(1)} %bitcast.84, bf16[256,4,64]{0,2,1:T(8,128)(2,1)S(1)} %bitcast.89, pred[1024]{0:T(1024)(128)(4,1)S(1)} %iota_compare_fusion.1, f32[]{:T(128)S(6)} %sqrt.3), kind=kOutput, calls=%fused_computation.13 | convolution fusion | flops 274857984 | bytes 1311748 | tf_op jit(solution)/shard_map/bgo,ogl->bgl/dot_general | solution.py:92
  68.9 2.3 %fusion.8 = f32[1,256]{1,0:T(1,128)} fusion(bf16[1024,1]{0,1:T(2,128)(2,1)S(1)} %reshape.226, f32[256,1024]{1,0:T(8,128)S(1)} %fusion.12, bf16[256,256]{0,1:T(8,128)(2,1)S(1)} %bitcast.101, bf16[512,1024]{1,0:T(8,128)(2,1)} %param.20), kind=kOutput, calls=%fused_computation.15 | convolution fusion | flops 136314880 | bytes 1707008 | tf_op jit(solution)/shard_map/dot_general | solution.py:104
  (19 shorter events, 0.2 us)
Async XLA Ops:
  6.5 38.5 %copy-start = (bf16[256,256]{1,0:T(8,128)(2,1)S(1)}, bf16[256,256]{1,0:T(8,128)(2,1)}, u32[]{:S(2)}) copy-start(bf16[256,256]{1,0:T(8,128)(2,1)} %param.17) | copy-start | bytes 393220
  16.0 9.8 %all-to-all-start = ((s32[4,1,320]{2,1,0:T(1,128)}), s32[4,1,320]{2,1,0:T(1,128)S(1)}, u32[]{:S(2)}, u32[]{:S(2)}) async-start(s32[4,1,320]{2,1,0:T(1,128)} %all_to_all.10), calls=%async_computation | async-start | bytes 12288 | tf_op jit(solution)/shard_map/all_to_all | solution.py:56
  21.2 44.4 %all-gather.2.cloned.1.call-start = ((), (), s32[]{:S(2)}) async-start(), calls=%async_computation.1 | async-start | bytes 1179648 | tf_op jit(solution)/shard_map/all_gather | solution.py:78
  31.9 10.3 %copy-start.4 = (bf16[256,256]{1,0:T(8,128)(2,1)S(1)}, bf16[256,256]{1,0:T(8,128)(2,1)}, u32[]{:S(2)}) copy-start(bf16[256,256]{1,0:T(8,128)(2,1)} %param.19) | copy-start | bytes 393220
  31.9 10.3 %copy-start.5 = (bf16[256,256]{1,0:T(8,128)(2,1)S(1)}, bf16[256,256]{1,0:T(8,128)(2,1)}, u32[]{:S(2)}) copy-start(bf16[256,256]{1,0:T(8,128)(2,1)} %param.18) | copy-start | bytes 393220
  31.9 11.9 %copy-start.3 = (bf16[1024]{0:T(1024)(128)(2,1)S(1)}, bf16[1024]{0:T(1024)(128)(2,1)}, u32[]{:S(2)}) copy-start(bf16[1024]{0:T(1024)(128)(2,1)} %param.21) | copy-start | bytes 6148
  31.9 11.9 %copy-start.2 = (s32[1,256,1]{1,2,0:T(1,128)S(1)}, s32[1,256,1]{1,2,0:T(1,128)}, u32[]{:S(2)}) copy-start(s32[1,256,1]{1,2,0:T(1,128)} %param.14) | copy-start | bytes 3076
  31.9 13.4 %copy-start.1 = (bf16[512,1024]{1,0:T(8,128)(2,1)S(1)}, bf16[512,1024]{1,0:T(8,128)(2,1)}, u32[]{:S(2)}) copy-start(bf16[512,1024]{1,0:T(8,128)(2,1)} %param.20) | copy-start | bytes 3145732
  32.3 7.4 %collective-permute-start.2 = (bf16[1,320,256]{2,1,0:T(8,128)(2,1)S(1)}, bf16[1,320,256]{2,1,0:T(8,128)(2,1)S(1)}, u32[]{:S(2)}, u32[]{:S(2)}) collective-permute-start(bf16[1,320,256]{2,1,0:T(8,128)(2,1)S(1)} %get-tuple-element.8), channel_id=1, source_target_pairs={{0,24},{8,16},{16,8},{24,0},{1,25},{9,17},{17,9},{25,1},{2,26},{10... | collective-permute-start | bytes 491528 | tf_op jit(solution)/shard_map/ppermute | solution.py:63
  32.9 7.7 %collective-permute-start.1 = (bf16[1,320,256]{2,1,0:T(8,128)(2,1)S(1)}, bf16[1,320,256]{2,1,0:T(8,128)(2,1)S(1)}, u32[]{:S(2)}, u32[]{:S(2)}) collective-permute-start(bf16[1,320,256]{2,1,0:T(8,128)(2,1)S(1)} %get-tuple-element.9), channel_id=1, source_target_pairs={{0,16},{8,24},{16,0},{24,8},{1,17},{9,25},{17,1},{25,9},{2,18},{10... | collective-permute-start | bytes 491528 | tf_op jit(solution)/shard_map/ppermute | solution.py:63
  34.4 6.3 %collective-permute-start = (bf16[1,320,256]{2,1,0:T(8,128)(2,1)S(1)}, bf16[1,320,256]{2,1,0:T(8,128)(2,1)S(1)}, u32[]{:S(2)}, u32[]{:S(2)}) collective-permute-start(bf16[1,320,256]{2,1,0:T(8,128)(2,1)S(1)} %get-tuple-element.10), channel_id=1, source_target_pairs={{0,8},{8,0},{16,24},{24,16},{1,9},{9,1},{17,25},{25,17},{2,10},{10... | collective-permute-start | bytes 491528 | tf_op jit(solution)/shard_map/ppermute | solution.py:63
Sparse Core Ops, SparseCore 0:
  43.2 22.3 all-gather.1
